TPU v7x, 512 devices: a whole 4x8x8 slice. The times are simulated.
512 devices in a mesh: pipe: 4 (over z_hi), ctx: 32 (over y, z_lo, core), dp: 4 (over x).
Axes of the slice: x: 4, y: 8, z: 8 (z_hi: 4, z_lo: 2; z = z_hi * 2 + z_lo), core: 2. Of those that a mesh axis runs over, the one named last changes fastest.
Arguments:
- queries: bfloat16 [4, 4, 4096, 4096], P('pipe', 'dp', 'ctx'), may hold values from -7 to 7
- key_input: bfloat16 [4, 4, 4096, 512], P('pipe', 'dp', 'ctx'), may hold values from -4 to 4
- value_input: bfloat16 [4, 4, 4096, 512], P('pipe', 'dp', 'ctx'), may hold values from -6 to 6
- incoming: bfloat16 [4, 4, 4096, 4096], P('pipe', 'dp', 'ctx'), may hold values from -6 to 6
- segments: int32 [4, 4096], P('dp'), may hold values from 0 to 15, never falling along the last dimension, each value on 1 to 512 neighbouring positions
Outputs:
- query_grad: bfloat16 [4, 4, 4096, 4096], P('pipe', 'dp', 'ctx')
- key_grad: bfloat16 [4, 4, 4096, 512], P('pipe', 'dp', 'ctx')
- value_grad: bfloat16 [4, 4, 4096, 512], P('pipe', 'dp', 'ctx')
- bias_grad: float32 [4, 5120], P('pipe')
Inputs may be any that keep to these rules, and one draw needn't show every extreme that they name: `segments`: tokens of one document are contiguous; every document holds 1 to 512 tokens and one holds exactly 512.
All inputs are finite; a program needn't handle non-finite values.
Results may differ from a plain program's by a relative error of at most 0.009.
Values may be sent and summed in bfloat16 or wider, within the bound.
No kernel may reach another device: no remote copies, remote signals or barrier semaphores. Data moves between devices by JAX's collectives and lax.ppermute only.
A program may use at most 64 MiB of HBM per device.

v0:
```python
import math
import jax
import jax.numpy as jnp
from jax import lax
from jax.sharding import PartitionSpec as P

ASKER_STREAMS = 32
SHARED_GROUPS = 4
FEATURE_SIZE = 128
QUERY_PER_KEY = 8


def passed_along(value, axis, steps):
    count = lax.axis_size(axis)
    pairs = [(source, (source + steps) % count) for source in range(count)]
    return lax.ppermute(value, axis, pairs)


def attend(
    queries, key_rows, value_rows, cotangent, query_doc, key_doc, query_pos, key_pos, scaling
):
    scores = (
        jnp.einsum("gqd,kd->gqk", queries, key_rows, preferred_element_type=jnp.float32) * scaling
    )
    visible = (query_doc[:, None] == key_doc[None, :]) & (key_pos[None, :] <= query_pos[:, None])
    scores = jnp.where(visible[None], scores, -1e30)
    row_max = jnp.max(scores, axis=-1, keepdims=True)
    weights = jnp.where(visible[None], jnp.exp(scores - row_max), 0.0)
    probs = weights / jnp.sum(weights, axis=-1, keepdims=True)
    probs_b = probs.astype(jnp.bfloat16)
    attn_out = jnp.einsum("gqk,kd->gqd", probs_b, value_rows, preferred_element_type=jnp.float32)
    dot_out = jnp.sum(cotangent.astype(jnp.float32) * attn_out, axis=-1, keepdims=True)
    grad_prob = jnp.einsum("gqd,kd->gqk", cotangent, value_rows, preferred_element_type=jnp.float32)
    grad_score = (probs * (grad_prob - dot_out) * scaling).astype(jnp.bfloat16)
    asker_derivative = jnp.einsum(
        "gqk,kd->gqd", grad_score, key_rows, preferred_element_type=jnp.float32
    )
    lookup_derivative = jnp.einsum(
        "gqk,gqd->kd", grad_score, queries, preferred_element_type=jnp.float32
    )
    content_derivative = jnp.einsum(
        "gqk,gqd->kd", probs_b, cotangent, preferred_element_type=jnp.float32
    )
    return (asker_derivative, lookup_derivative, content_derivative)


def banded(queries, key_rows, value_rows, cotangent, doc_ids, block_len, scaling):
    length = doc_ids.shape[0]
    blocks = length // block_len
    width = key_rows.shape[1]
    key_pad = jnp.concatenate([jnp.zeros((block_len, width), key_rows.dtype), key_rows], axis=0)
    value_pad = jnp.concatenate(
        [jnp.zeros((block_len, width), value_rows.dtype), value_rows], axis=0
    )
    doc_pad = jnp.concatenate([jnp.full((block_len,), -1, jnp.int32), doc_ids])
    pos_pad = jnp.arange(length + block_len, dtype=jnp.int32) - block_len

    def step(carried, block):
        key_acc, value_acc = carried
        anchor = block * block_len
        query_blk = lax.dynamic_slice_in_dim(queries, anchor, block_len, 1)
        cot_blk = lax.dynamic_slice_in_dim(cotangent, anchor, block_len, 1)
        key_blk = lax.dynamic_slice_in_dim(key_pad, anchor, 2 * block_len, 0)
        value_blk = lax.dynamic_slice_in_dim(value_pad, anchor, 2 * block_len, 0)
        query_doc = lax.dynamic_slice_in_dim(doc_ids, anchor, block_len, 0)
        key_doc = lax.dynamic_slice_in_dim(doc_pad, anchor, 2 * block_len, 0)
        query_pos = anchor + jnp.arange(block_len, dtype=jnp.int32)
        key_pos = lax.dynamic_slice_in_dim(pos_pad, anchor, 2 * block_len, 0)
        asker_derivative, lookup_derivative, content_derivative = attend(
            query_blk, key_blk, value_blk, cot_blk, query_doc, key_doc, query_pos, key_pos, scaling
        )
        key_acc = lax.dynamic_update_slice_in_dim(
            key_acc,
            lax.dynamic_slice_in_dim(key_acc, anchor, 2 * block_len, 0) + lookup_derivative,
            anchor,
            0,
        )
        value_acc = lax.dynamic_update_slice_in_dim(
            value_acc,
            lax.dynamic_slice_in_dim(value_acc, anchor, 2 * block_len, 0) + content_derivative,
            anchor,
            0,
        )
        return ((key_acc, value_acc), asker_derivative)

    start_acc = jnp.zeros((length + block_len, width), jnp.float32)
    (key_acc, value_acc), query_blocks = lax.scan(
        step, (start_acc, start_acc), jnp.arange(blocks, dtype=jnp.int32)
    )
    groups = queries.shape[0]
    asker_derivative = query_blocks.transpose(1, 0, 2, 3).reshape(groups, length, width)
    return (asker_derivative, key_acc[block_len:], value_acc[block_len:])


def body(queries, key_input, value_input, incoming, segments):
    shard_length = queries.shape[2]
    ctx_size = lax.axis_size("ctx")
    reach_dev = min(4, ctx_size - 1)
    block_len = reach_dev * shard_length
    scaling = 1.0 / math.sqrt(FEATURE_SIZE)
    doc_ids = segments[0]
    handed = passed_along(incoming, "pipe", -1)
    query_tok = queries[0, 0].reshape(shard_length, ASKER_STREAMS, FEATURE_SIZE)
    cot_tok = handed[0, 0].reshape(shard_length, ASKER_STREAMS, FEATURE_SIZE)
    key_widened = jnp.repeat(
        key_input[0, 0].reshape(shard_length, SHARED_GROUPS, FEATURE_SIZE), QUERY_PER_KEY, axis=1
    )
    value_widened = jnp.repeat(
        value_input[0, 0].reshape(shard_length, SHARED_GROUPS, FEATURE_SIZE), QUERY_PER_KEY, axis=1
    )
    query_head, key_head, value_head, cot_head = (
        lax.all_to_all(query_tok, "ctx", split_axis=1, concat_axis=0, tiled=True),
        lax.all_to_all(key_widened, "ctx", split_axis=1, concat_axis=0, tiled=True),
        lax.all_to_all(value_widened, "ctx", split_axis=1, concat_axis=0, tiled=True),
        lax.all_to_all(cot_tok, "ctx", split_axis=1, concat_axis=0, tiled=True),
    )

    def per_head(members):
        return banded(
            members[0][None], members[1], members[2], members[3][None], doc_ids, block_len, scaling
        )

    asker_derivative, lookup_derivative, content_derivative = lax.map(
        per_head,
        (
            query_head.transpose(1, 0, 2),
            key_head.transpose(1, 0, 2),
            value_head.transpose(1, 0, 2),
            cot_head.transpose(1, 0, 2),
        ),
    )
    asker_derivative = asker_derivative[:, 0].transpose(1, 0, 2)
    lookup_derivative = lookup_derivative.transpose(1, 0, 2)
    content_derivative = content_derivative.transpose(1, 0, 2)
    query_back, key_backward, value_backward = (
        lax.all_to_all(asker_derivative, "ctx", split_axis=0, concat_axis=1, tiled=True),
        lax.all_to_all(lookup_derivative, "ctx", split_axis=0, concat_axis=1, tiled=True),
        lax.all_to_all(content_derivative, "ctx", split_axis=0, concat_axis=1, tiled=True),
    )
    query_flat = query_back.reshape(shard_length, ASKER_STREAMS * FEATURE_SIZE)
    key_flattened = (
        key_backward.reshape(shard_length, SHARED_GROUPS, QUERY_PER_KEY, FEATURE_SIZE)
        .sum(axis=2)
        .reshape(shard_length, SHARED_GROUPS * FEATURE_SIZE)
    )
    value_flat = (
        value_backward.reshape(shard_length, SHARED_GROUPS, QUERY_PER_KEY, FEATURE_SIZE)
        .sum(axis=2)
        .reshape(shard_length, SHARED_GROUPS * FEATURE_SIZE)
    )
    offset_parts = jnp.concatenate(
        [jnp.sum(query_flat, axis=0), jnp.sum(key_flattened, axis=0), jnp.sum(value_flat, axis=0)]
    )
    pipe_idx = lax.axis_index("pipe")
    slots = (
        jnp.zeros((lax.axis_size("pipe"), offset_parts.shape[0]), jnp.float32)
        .at[pipe_idx]
        .set(offset_parts)
    )
    offset_overall = lax.psum(slots, ("pipe", "ctx", "dp"))[pipe_idx]
    bias_scaled = offset_overall / math.sqrt(lax.axis_size("dp") * shard_length * ctx_size)
    query_grad = query_flat.astype(jnp.bfloat16)[None, None]
    key_grad = key_flattened.astype(jnp.bfloat16)[None, None]
    value_grad = value_flat.astype(jnp.bfloat16)[None, None]
    return (query_grad, key_grad, value_grad, bias_scaled[None])


def solution(mesh):
    return jax.shard_map(
        body,
        mesh=mesh,
        in_specs=(
            P("pipe", "dp", "ctx", None),
            P("pipe", "dp", "ctx", None),
            P("pipe", "dp", "ctx", None),
            P("pipe", "dp", "ctx", None),
            P("dp", None),
        ),
        out_specs=(
            P("pipe", "dp", "ctx", None),
            P("pipe", "dp", "ctx", None),
            P("pipe", "dp", "ctx", None),
            P("pipe", None),
        ),
        check_vma=False,
    )
```

profile of v0, /device:TPU:1, one launch (start us, length us, event | category | flops | bytes accessed | tf_op | source)
XLA Modules:
  0.0 760.0 jit_solution(13099326957965084261)
XLA Ops:
  9.4 10.6 %all-to-all-start.1 = ((bf16[128,32,128]{2,0,1:T(8,128)(2,1)}), bf16[128,32,128]{2,0,1:T(8,128)(2,1)S(1)}, u32[]{:S(2)}, u32[]{:S(2)}) async-start(bf16[128,32,128]{2,0,1:T(8,128)(2,1)} %bitcast.9), calls=%async_computation.1 | async-start | bytes 2097152 | tf_op jit(solution)/shard_map/all_to_all | solution.py:113
  20.0 28.0 %all-to-all-done.1 = bf16[128,32,128]{2,0,1:T(8,128)(2,1)S(1)} async-done(((bf16[128,32,128]{2,0,1:T(8,128)(2,1)}), bf16[128,32,128]{2,0,1:T(8,128)(2,1)S(1)}, u32[]{:S(2)}, u32[]{:S(2)}) %all-to-all-start.1) | async-done | bytes 1048608 | tf_op jit(solution)/shard_map/all_to_all | solution.py:113
  49.2 4.3 all-to-all-start.3
  53.6 9.8 %collective-permute-start = (bf16[1,1,128,4096]{3,2,1,0:T(8,128)(2,1)}, bf16[1,1,128,4096]{3,2,1,0:T(8,128)(2,1)S(1)}, u32[]{:S(2)}, u32[]{:S(2)}) collective-permute-start(bf16[1,1,128,4096]{3,2,1,0:T(8,128)(2,1)} %param.12), channel_id=1, source_target_pairs={{0,384},{128,0},{256,128},{384,256},{1,385},{129,1},{257,129},{385... | collective-permute-start | bytes 3145736 | tf_op jit(solution)/shard_map/ppermute | solution.py:16
  63.3 54.2 %collective-permute-done = bf16[1,1,128,4096]{3,2,1,0:T(8,128)(2,1)S(1)} collective-permute-done((bf16[1,1,128,4096]{3,2,1,0:T(8,128)(2,1)}, bf16[1,1,128,4096]{3,2,1,0:T(8,128)(2,1)S(1)}, u32[]{:S(2)}, u32[]{:S(2)}) %collective-permute-start) | collective-permute-done | bytes 1048608 | tf_op jit(solution)/shard_map/ppermute | solution.py:16
  118.9 6.5 all-to-all-start.2
  128.2 25.2 %all-to-all-done.2 = bf16[128,32,128]{0,2,1:T(8,128)(2,1)S(1)} async-done(((bf16[128,32,128]{0,2,1:T(8,128)(2,1)}), bf16[128,32,128]{0,2,1:T(8,128)(2,1)S(1)}, u32[]{:S(2)}, u32[]{:S(2)}) %all-to-all-start.2) | async-done | bytes 1048608 | tf_op jit(solution)/shard_map/all_to_all | solution.py:115
  153.5 5.0 all-to-all-start
  162.2 24.3 %all-to-all-done = bf16[128,32,128]{2,0,1:T(8,128)(2,1)} async-done(((bf16[128,32,128]{2,0,1:T(8,128)(2,1)}), bf16[128,32,128]{2,0,1:T(8,128)(2,1)}, u32[]{:S(2)}, u32[]{:S(2)}) %all-to-all-start) | async-done | bytes 1048608 | tf_op jit(solution)/shard_map/all_to_all | solution.py:112
  190.1 126.4 %while.26 = (s32[]{:T(128)}, f32[4608,128]{1,0:T(8,128)}, f32[4608,128]{1,0:T(8,128)}, f32[8,1,512,128]{3,2,1,0:T(8,128)}, s32[8]{0:T(128)}, /*index=5*/s32[4096...) while((s32[]{:T(128)}, f32[4608,128]{1,0:T(8,128)}, ...), condition=%wide.region_4.5_spmd, body=%wide.region_0.4_spmd.sunk | while | flops 820444160 | bytes 22487344 | solution.py:87
  199.1 2.4 fusion.59
  201.5 2.3 fusion.60
  214.9 2.4 fusion.59
  217.3 2.3 fusion.60
  230.7 2.4 fusion.59
  233.1 2.3 fusion.60
  246.5 2.4 fusion.59
  262.3 2.4 fusion.59
  264.7 2.3 fusion.60
  278.1 2.4 fusion.59
  280.5 2.3 fusion.60
  293.9 2.4 fusion.59
  296.3 2.3 fusion.60
  309.7 2.4 fusion.59
  312.1 2.3 fusion.60
  316.5 3.1 slice.22
  319.7 6.0 all-to-all-start.5
  327.1 48.6 %all-to-all-done.5 = f32[4096,1,128]{2,1,0:T(1,128)} async-done(((f32[4096,1,128]{2,1,0:T(1,128)}), f32[4096,1,128]{2,1,0:T(1,128)}, u32[]{:S(2)}, u32[]{:S(2)}) %all-to-all-start.5) | async-done | bytes 2097184 | tf_op jit(solution)/shard_map/all_to_all | solution.py:137
  375.7 56.1 %all_to_all.105 = f32[4096,1,128]{2,1,0:T(1,128)S(1)} all-to-all(f32[4096,1,128]{2,1,0:T(1,128)} %bitcast.107), channel_id=1, replica_groups=mesh['pipe'=4,'ctx'=32,'dp'=4] {'ctx'}, dimensions={0} | all-to-all | bytes 4194304 | tf_op jit(solution)/shard_map/all_to_all | solution.py:138
  431.9 6.0 all-to-all-start.4
  440.6 47.4 %all-to-all-done.4 = f32[4096,1,128]{2,1,0:T(1,128)} async-done(((f32[4096,1,128]{2,1,0:T(1,128)}), f32[4096,1,128]{2,1,0:T(1,128)}, u32[]{:S(2)}, u32[]{:S(2)}) %all-to-all-start.4) | async-done | bytes 2097184 | tf_op jit(solution)/shard_map/all_to_all | solution.py:136
  500.4 251.3 %all-reduce.5.cloned.1.call-done = f32[4,5120]{1,0:T(4,128)} async-done(((f32[4,5120]{1,0:T(4,128)}), f32[4,5120]{1,0:T(4,128)}) %all-reduce.5.cloned.1.call-update) | async-done | bytes 81936 | tf_op jit(solution)/shard_map/psum | solution.py:160
  (156 shorter events, 119.1 us)
Async XLA Ops:
  7.2 12.8 %copy-start.2 = (bf16[1,1,128,512]{3,2,1,0:T(8,128)(2,1)S(1)}, bf16[1,1,128,512]{3,2,1,0:T(8,128)(2,1)}, u32[]{:S(2)}) copy-start(bf16[1,1,128,512]{3,2,1,0:T(8,128)(2,1)} %param.11) | copy-start | bytes 393220
  9.4 38.6 %all-to-all-start.1 = ((bf16[128,32,128]{2,0,1:T(8,128)(2,1)}), bf16[128,32,128]{2,0,1:T(8,128)(2,1)S(1)}, u32[]{:S(2)}, u32[]{:S(2)}) async-start(bf16[128,32,128]{2,0,1:T(8,128)(2,1)} %bitcast.9), calls=%async_computation.1 | async-start | bytes 2097152 | tf_op jit(solution)/shard_map/all_to_all | solution.py:113
  49.2 69.6 %all-to-all-start.3 = ((bf16[128,32,128]{2,0,1:T(8,128)(2,1)}), bf16[128,32,128]{2,0,1:T(8,128)(2,1)S(1)}, u32[]{:S(2)}, u32[]{:S(2)}) async-start(bf16[128,32,128]{2,0,1:T(8,128)(2,1)} %bitcast.17), calls=%async_computation.3 | async-start | bytes 2097152 | tf_op jit(solution)/shard_map/all_to_all | solution.py:114
  53.6 64.0 %collective-permute-start = (bf16[1,1,128,4096]{3,2,1,0:T(8,128)(2,1)}, bf16[1,1,128,4096]{3,2,1,0:T(8,128)(2,1)S(1)}, u32[]{:S(2)}, u32[]{:S(2)}) collective-permute-start(bf16[1,1,128,4096]{3,2,1,0:T(8,128)(2,1)} %param.12), channel_id=1, source_target_pairs={{0,384},{128,0},{256,128},{384,256},{1,385},{129,1},{257,129},{385... | collective-permute-start | bytes 3145736 | tf_op jit(solution)/shard_map/ppermute | solution.py:16
  118.9 34.6 %all-to-all-start.2 = ((bf16[128,32,128]{0,2,1:T(8,128)(2,1)}), bf16[128,32,128]{0,2,1:T(8,128)(2,1)S(1)}, u32[]{:S(2)}, u32[]{:S(2)}) async-start(bf16[128,32,128]{0,2,1:T(8,128)(2,1)} %bitcast.110), calls=%async_computation.2 | async-start | bytes 2097152 | tf_op jit(solution)/shard_map/all_to_all | solution.py:115
  126.8 31.6 %copy-start.3 = (s32[1,4096]{1,0:T(1,128)S(1)}, s32[1,4096]{1,0:T(1,128)}, u32[]{:S(2)}) copy-start(s32[1,4096]{1,0:T(1,128)} %param.13) | copy-start | bytes 49156
  153.5 33.0 %all-to-all-start = ((bf16[128,32,128]{2,0,1:T(8,128)(2,1)}), bf16[128,32,128]{2,0,1:T(8,128)(2,1)}, u32[]{:S(2)}, u32[]{:S(2)}) async-start(bf16[128,32,128]{2,0,1:T(8,128)(2,1)} %copy.41), calls=%async_computation | async-start | bytes 2097152 | tf_op jit(solution)/shard_map/all_to_all | solution.py:112
  319.7 6.0 copy-start
  319.7 56.1 %all-to-all-start.5 = ((f32[4096,1,128]{2,1,0:T(1,128)}), f32[4096,1,128]{2,1,0:T(1,128)}, u32[]{:S(2)}, u32[]{:S(2)}) async-start(f32[4096,1,128]{2,1,0:T(1,128)} %bitcast.106), calls=%async_computation.5 | async-start | bytes 4194304 | tf_op jit(solution)/shard_map/all_to_all | solution.py:137
  431.9 6.1 copy-start.4
  431.9 56.1 %all-to-all-start.4 = ((f32[4096,1,128]{2,1,0:T(1,128)}), f32[4096,1,128]{2,1,0:T(1,128)}, u32[]{:S(2)}, u32[]{:S(2)}) async-start(f32[4096,1,128]{2,1,0:T(1,128)} %bitcast.114), calls=%async_computation.4 | async-start | bytes 4194304 | tf_op jit(solution)/shard_map/all_to_all | solution.py:136
  437.9 313.8 %all-reduce.5.cloned.1.call-start = ((), (), s32[]{:S(2)}) async-start(), calls=%async_computation.7 | async-start | bytes 163840 | tf_op jit(solution)/shard_map/psum | solution.py:160
  490.7 0.6 copy-start.1
Sparse Core Ops, SparseCore 0:
  491.5 260.1 all-reduce.4
where the time goes:
time: 763 us; the launch traced here: 760 us
  waiting for transfers between devices  479 us (63%)
  matrix products  76.2 us (10%)
  local copies, waits for them, and re-layouts  56.1 us (7%)
  blocking collectives  56.1 us (7%)
  starting transfers between devices  48.2 us (6%)
  other arithmetic  25.3 us (3%)
  between operations  14.3 us (2%)
    psum x1, waiting for transfers between devices, body(): offset_overall = lax.psum(slots, ('pipe', 'ctx', 'dp'))[pipe_idx]  251 us
    all_to_all x1, blocking collectives, body(): lax.all_to_all(content_derivative, 'ctx', split_axis=0, concat_axis=1, ti...  56.1 us
    ppermute x1, waiting for transfers between devices, passed_along(): return lax.ppermute(value, axis, pairs)  54.2 us
    all_to_all x1, waiting for transfers between devices, body(): lax.all_to_all(lookup_derivative, 'ctx', split_axis=0, concat_axis=1, til...  48.6 us
    all_to_all x1, waiting for transfers between devices, body(): lax.all_to_all(asker_derivative, 'ctx', split_axis=0, concat_axis=1, tile...  47.4 us
    all_to_all x1, waiting for transfers between devices, body(): lax.all_to_all(key_widened, 'ctx', split_axis=1, concat_axis=0, tiled=True)  28 us
    all_to_all x1, waiting for transfers between devices, body(): lax.all_to_all(cot_tok, 'ctx', split_axis=1, concat_axis=0, tiled=True)  25.2 us
    all_to_all x1, waiting for transfers between devices, body(): lax.all_to_all(query_tok, 'ctx', split_axis=1, concat_axis=0, tiled=True)  24.3 us
  transfers between devices with their start and end apart: 8, of which 7 were waited for; matrix products, arithmetic and copies ran while one was open for 3% of the time, Pallas kernels for 0%

commit v1 on v0

--- a/solution.py
+++ b/solution.py
@@ -1,3 +1,4 @@
+import functools
 import math
 import jax
 import jax.numpy as jnp
@@ -8,6 +9,13 @@
 SHARED_GROUPS = 4
 FEATURE_SIZE = 128
 QUERY_PER_KEY = 8
+
+
+def raise_slabs(vec, axis_key):
+    return jnp.sum(lax.all_gather(vec, axis_key), 0)
+
+
+guide_the_region = functools.partial(raise_slabs, axis_key=("pipe", "ctx", "dp"))
 
 
 def passed_along(value, axis, steps):
@@ -157,7 +165,7 @@
         .at[pipe_idx]
         .set(offset_parts)
     )
-    offset_overall = lax.psum(slots, ("pipe", "ctx", "dp"))[pipe_idx]
+    offset_overall = guide_the_region(slots)[pipe_idx]
     bias_scaled = offset_overall / math.sqrt(lax.axis_size("dp") * shard_length * ctx_size)
     query_grad = query_flat.astype(jnp.bfloat16)[None, None]
     key_grad = key_flattened.astype(jnp.bfloat16)[None, None]

time: 763 us -> 1990 us (2.61)
  waiting for transfers between devices: 479 us -> 1690 us
    all_gather x0 -> x1, waiting for transfers between devices: none -> 1460 us  [raise_slabs(): return jnp.sum(lax.all_gather(vec, axis_key), 0)]
    psum x1 -> x0, waiting for transfers between devices: 251 us -> none  [body(): offset_overall = lax.psum(slots, ('pipe', 'ctx', 'dp'))[pipe_idx]]
  transfers between devices with their start and end apart: 8 -> 8, of which waited for: 7 -> 7; matrix products, arithmetic and copies ran while one was open for 3% -> 1% of each run, Pallas kernels for 0% -> 0%
where the time goes in v1:
time: 1990 us; the launch traced here: 1980 us
  waiting for transfers between devices  1690 us (85%)
  matrix products  76.2 us (4%)
  local copies, waits for them, and re-layouts  56.2 us (3%)
  blocking collectives  56.1 us (3%)
  starting transfers between devices  48.2 us (2%)
  other arithmetic  38.6 us (2%)
    all_gather x1, waiting for transfers between devices, raise_slabs(): return jnp.sum(lax.all_gather(vec, axis_key), 0)  1460 us
    all_to_all x1, blocking collectives, body(): lax.all_to_all(content_derivative, 'ctx', split_axis=0, concat_axis=1, ti...  56.1 us
    ppermute x1, waiting for transfers between devices, passed_along(): return lax.ppermute(value, axis, pairs)  54.2 us
    all_to_all x1, waiting for transfers between devices, body(): lax.all_to_all(lookup_derivative, 'ctx', split_axis=0, concat_axis=1, til...  48.6 us
    all_to_all x1, waiting for transfers between devices, body(): lax.all_to_all(asker_derivative, 'ctx', split_axis=0, concat_axis=1, tile...  47.4 us
  transfers between devices with their start and end apart: 8, of which 7 were waited for; matrix products, arithmetic and copies ran while one was open for 1% of the time, Pallas kernels for 0%

profile of v1, /device:TPU:1, one launch (start us, length us, event | category | flops | bytes accessed | tf_op | source)
XLA Modules:
  0.0 1981.0 jit_solution(7645943773810092349)
XLA Ops:
  9.4 10.6 all-to-all-start.1
  20.0 28.0 %all-to-all-done.1 = bf16[128,32,128]{2,0,1:T(8,128)(2,1)S(1)} async-done(((bf16[128,32,128]{2,0,1:T(8,128)(2,1)}), bf16[128,32,128]{2,0,1:T(8,128)(2,1)S(1)}, u32[]{:S(2)}, u32[]{:S(2)}) %all-to-all-start.1) | async-done | bytes 1048608 | tf_op jit(solution)/shard_map/all_to_all | solution.py:121
  49.2 4.3 all-to-all-start.3
  53.6 9.8 collective-permute-start
  63.3 54.2 %collective-permute-done = bf16[1,1,128,4096]{3,2,1,0:T(8,128)(2,1)S(1)} collective-permute-done((bf16[1,1,128,4096]{3,2,1,0:T(8,128)(2,1)}, bf16[1,1,128,4096]{3,2,1,0:T(8,128)(2,1)S(1)}, u32[]{:S(2)}, u32[]{:S(2)}) %collective-permute-start) | collective-permute-done | bytes 1048608 | tf_op jit(solution)/shard_map/ppermute | solution.py:24
  118.9 6.5 all-to-all-start.2
  128.2 25.2 %all-to-all-done.2 = bf16[128,32,128]{0,2,1:T(8,128)(2,1)S(1)} async-done(((bf16[128,32,128]{0,2,1:T(8,128)(2,1)}), bf16[128,32,128]{0,2,1:T(8,128)(2,1)S(1)}, u32[]{:S(2)}, u32[]{:S(2)}) %all-to-all-start.2) | async-done | bytes 1048608 | tf_op jit(solution)/shard_map/all_to_all | solution.py:123
  153.5 5.0 all-to-all-start
  162.2 24.3 %all-to-all-done = bf16[128,32,128]{2,0,1:T(8,128)(2,1)} async-done(((bf16[128,32,128]{2,0,1:T(8,128)(2,1)}), bf16[128,32,128]{2,0,1:T(8,128)(2,1)}, u32[]{:S(2)}, u32[]{:S(2)}) %all-to-all-start) | async-done | bytes 1048608 | tf_op jit(solution)/shard_map/all_to_all | solution.py:120
  190.1 126.4 %while.26 = (s32[]{:T(128)}, f32[4608,128]{1,0:T(8,128)}, f32[4608,128]{1,0:T(8,128)}, f32[8,1,512,128]{3,2,1,0:T(8,128)}, s32[8]{0:T(128)}, /*index=5*/s32[4096...) while((s32[]{:T(128)}, f32[4608,128]{1,0:T(8,128)}, ...), condition=%wide.region_4.5_spmd, body=%wide.region_0.4_spmd.sunk | while | flops 820444160 | bytes 22487344 | solution.py:95
  199.1 2.4 fusion.59
  201.5 2.3 fusion.60
  214.9 2.4 fusion.59
  217.3 2.3 fusion.60
  230.7 2.4 fusion.59
  233.1 2.3 fusion.60
  246.5 2.4 fusion.59
  262.3 2.4 fusion.59
  264.7 2.3 fusion.60
  278.1 2.4 fusion.59
  280.5 2.3 fusion.60
  293.9 2.4 fusion.59
  296.3 2.3 fusion.60
  309.7 2.4 fusion.59
  316.5 3.1 slice.22
  319.7 6.0 all-to-all-start.5
  327.2 48.6 %all-to-all-done.5 = f32[4096,1,128]{2,1,0:T(1,128)} async-done(((f32[4096,1,128]{2,1,0:T(1,128)}), f32[4096,1,128]{2,1,0:T(1,128)}, u32[]{:S(2)}, u32[]{:S(2)}) %all-to-all-start.5) | async-done | bytes 2097184 | tf_op jit(solution)/shard_map/all_to_all | solution.py:145
  375.7 56.1 %all_to_all.105 = f32[4096,1,128]{2,1,0:T(1,128)S(1)} all-to-all(f32[4096,1,128]{2,1,0:T(1,128)} %bitcast.107), channel_id=1, replica_groups=mesh['pipe'=4,'ctx'=32,'dp'=4] {'ctx'}, dimensions={0} | all-to-all | bytes 4194304 | tf_op jit(solution)/shard_map/all_to_all | solution.py:146
  431.9 6.0 all-to-all-start.4
  440.6 47.4 %all-to-all-done.4 = f32[4096,1,128]{2,1,0:T(1,128)} async-done(((f32[4096,1,128]{2,1,0:T(1,128)}), f32[4096,1,128]{2,1,0:T(1,128)}, u32[]{:S(2)}, u32[]{:S(2)}) %all-to-all-start.4) | async-done | bytes 2097184 | tf_op jit(solution)/shard_map/all_to_all | solution.py:144
  500.4 1459.1 %all-gather.2.cloned.1.call-done = f32[512,4,5120]{2,1,0:T(4,128)} async-done(((f32[1,4,5120]{2,1,0:T(4,128)}), f32[512,4,5120]{2,1,0:T(4,128)}) %all-gather.2.cloned.1.call-update) | async-done | bytes 41943056 | tf_op jit(solution)/shard_map/all_gather | solution.py:15
  1959.4 14.1 reduce_sum.95
  (157 shorter events, 120.5 us)
Async XLA Ops:
  7.2 12.8 copy-start.2
  9.4 38.6 %all-to-all-start.1 = ((bf16[128,32,128]{2,0,1:T(8,128)(2,1)}), bf16[128,32,128]{2,0,1:T(8,128)(2,1)S(1)}, u32[]{:S(2)}, u32[]{:S(2)}) async-start(bf16[128,32,128]{2,0,1:T(8,128)(2,1)} %bitcast.9), calls=%async_computation.1 | async-start | bytes 2097152 | tf_op jit(solution)/shard_map/all_to_all | solution.py:121
  49.2 69.6 %all-to-all-start.3 = ((bf16[128,32,128]{2,0,1:T(8,128)(2,1)}), bf16[128,32,128]{2,0,1:T(8,128)(2,1)S(1)}, u32[]{:S(2)}, u32[]{:S(2)}) async-start(bf16[128,32,128]{2,0,1:T(8,128)(2,1)} %bitcast.17), calls=%async_computation.3 | async-start | bytes 2097152 | tf_op jit(solution)/shard_map/all_to_all | solution.py:122
  53.6 64.0 %collective-permute-start = (bf16[1,1,128,4096]{3,2,1,0:T(8,128)(2,1)}, bf16[1,1,128,4096]{3,2,1,0:T(8,128)(2,1)S(1)}, u32[]{:S(2)}, u32[]{:S(2)}) collective-permute-start(bf16[1,1,128,4096]{3,2,1,0:T(8,128)(2,1)} %param.12), channel_id=1, source_target_pairs={{0,384},{128,0},{256,128},{384,256},{1,385},{129,1},{257,129},{385... | collective-permute-start | bytes 3145736 | tf_op jit(solution)/shard_map/ppermute | solution.py:24
  118.9 34.6 %all-to-all-start.2 = ((bf16[128,32,128]{0,2,1:T(8,128)(2,1)}), bf16[128,32,128]{0,2,1:T(8,128)(2,1)S(1)}, u32[]{:S(2)}, u32[]{:S(2)}) async-start(bf16[128,32,128]{0,2,1:T(8,128)(2,1)} %bitcast.110), calls=%async_computation.2 | async-start | bytes 2097152 | tf_op jit(solution)/shard_map/all_to_all | solution.py:123
  126.8 31.6 %copy-start.3 = (s32[1,4096]{1,0:T(1,128)S(1)}, s32[1,4096]{1,0:T(1,128)}, u32[]{:S(2)}) copy-start(s32[1,4096]{1,0:T(1,128)} %param.13) | copy-start | bytes 49156
  153.5 33.0 %all-to-all-start = ((bf16[128,32,128]{2,0,1:T(8,128)(2,1)}), bf16[128,32,128]{2,0,1:T(8,128)(2,1)}, u32[]{:S(2)}, u32[]{:S(2)}) async-start(bf16[128,32,128]{2,0,1:T(8,128)(2,1)} %copy.41), calls=%async_computation | async-start | bytes 2097152 | tf_op jit(solution)/shard_map/all_to_all | solution.py:120
  319.7 6.0 copy-start
  319.7 56.1 %all-to-all-start.5 = ((f32[4096,1,128]{2,1,0:T(1,128)}), f32[4096,1,128]{2,1,0:T(1,128)}, u32[]{:S(2)}, u32[]{:S(2)}) async-start(f32[4096,1,128]{2,1,0:T(1,128)} %bitcast.106), calls=%async_computation.5 | async-start | bytes 4194304 | tf_op jit(solution)/shard_map/all_to_all | solution.py:145
  431.9 6.1 copy-start.4
  431.9 56.1 %all-to-all-start.4 = ((f32[4096,1,128]{2,1,0:T(1,128)}), f32[4096,1,128]{2,1,0:T(1,128)}, u32[]{:S(2)}, u32[]{:S(2)}) async-start(f32[4096,1,128]{2,1,0:T(1,128)} %bitcast.114), calls=%async_computation.4 | async-start | bytes 4194304 | tf_op jit(solution)/shard_map/all_to_all | solution.py:144
  437.9 1521.5 %all-gather.2.cloned.1.call-start = ((), (), s32[]{:S(2)}) async-start(), calls=%async_computation.7 | async-start | bytes 42024960 | tf_op jit(solution)/shard_map/all_gather | solution.py:15
  490.7 0.6 copy-start.1
Sparse Core Ops, SparseCore 0:
  491.5 1467.8 all-gather.1
